TPU v7x, 256 devices: a whole 4x4x8 slice. The times are simulated.
256 devices in a mesh: req: 32 (over y, z), head: 8 (over x, core).
Axes of the slice: x: 4, y: 4, z: 8, core: 2. Of those that a mesh axis runs over, the one named last changes fastest.
Arguments:
- tokens: bfloat16 [32768, 1024], P(('req', 'head')), may hold values from -6 to 6
- w_proj: bfloat16 [1024, 2048], P(None, 'head'), may hold values from -0.1875 to 0.1875
- w_out: bfloat16 [1024, 1024], replicated, may hold values from -0.1875 to 0.1875
- kv_cache: bfloat16 [32, 32, 3, 128, 2048], P('req', None, None, None, 'head'), may hold values from -6 to 6
- slot_request: int32 [64], P('req'), may hold values from 0 to 63, each once
- lengths: int32 [64], replicated, may hold values from 1 to 4096
- block_owner: int32 [2048, 1], P('req'), may hold values from 0 to 31; in each aligned block of 64 rows (0 to 63, 64 to 127, ...) at most 3 rows name the same one
Outputs:
- mixed: bfloat16 [32768, 1024], P(('req', 'head'))
Inputs may be any that keep to these rules, and one draw needn't show every extreme that they name: `block_owner`: within each aligned block of 64 rows no owner appears more than 3 times.
All inputs are finite; a program needn't handle non-finite values.
Results may differ from a plain program's by a relative error of at most 0.0088.
Values may be sent and summed in bfloat16 or wider, within the bound.
No kernel may reach another device: no remote copies, remote signals or barrier semaphores. Data moves between devices by JAX's collectives and lax.ppermute only.
A program may use at most 128 MiB of HBM per device.

v0:
```python
import jax
import jax.numpy as jnp
from jax import lax
from jax.sharding import PartitionSpec as P

DH = 64
CAND = 512
BLK = 128
MAXB = 32


def layer_norm(values):
    mean = jnp.mean(values, axis=-1, keepdims=True)
    square = jnp.mean(values * values, axis=-1, keepdims=True)
    return (values - mean) * lax.rsqrt(square - mean * mean + 1e-05)


def shards(tokens, w_proj, w_out, kv_cache, slot_request, lengths, block_owner):
    head_local = w_proj.shape[1] // (2 * DH)
    gathered = lax.all_gather(tokens, "head", axis=0, tiled=True)
    normed = layer_norm(gathered.astype(jnp.float32)).astype(jnp.bfloat16)
    row_count = normed.shape[0]
    slots = row_count // CAND
    proj = jax.nn.silu(jnp.dot(normed, w_proj, preferred_element_type=jnp.float32))
    proj = proj.reshape(row_count, head_local, 2, DH)
    gate_u = proj[:, :, 0].astype(jnp.bfloat16).reshape(row_count, head_local * DH)
    query = proj[:, :, 1].astype(jnp.bfloat16).reshape(slots, CAND, head_local, DH)
    received = lax.all_to_all(kv_cache, "req", split_axis=1, concat_axis=0, tiled=True)
    most_slots = received.shape[2]
    pool = received.reshape(-1, BLK, received.shape[-1])
    owner_count = lax.axis_size("req")
    owners = block_owner[:, 0]
    onehot = (owners[:, None] == jnp.arange(owner_count, dtype=jnp.int32)[None, :]).astype(
        jnp.int32
    )
    rank = jnp.sum((jnp.cumsum(onehot, axis=0) - onehot) * onehot, axis=1)
    history = pool[owners * most_slots + rank].reshape(slots, MAXB * BLK, head_local, 2, DH)
    total_requests = lengths.shape[0]
    match = slot_request[:, None] == jnp.arange(total_requests, dtype=jnp.int32)[None, :]
    slot_lengths = jnp.sum(jnp.where(match, lengths[None, :], 0), axis=1)
    positions = jnp.arange(MAXB * BLK, dtype=jnp.int32)
    scale = 1.0 / DH**0.5
    results = []
    for slot in range(slots):
        keys = history[slot, :, :, 0]
        values = history[slot, :, :, 1]
        scores = (
            jnp.einsum("chd,phd->hcp", query[slot], keys, preferred_element_type=jnp.float32)
            * scale
        )
        live = positions < slot_lengths[slot]
        weights = jnp.where(live[None, None, :], jax.nn.silu(scores), 0.0).astype(jnp.bfloat16)
        results.append(
            jnp.einsum("hcp,phd->chd", weights, values, preferred_element_type=jnp.float32)
        )
    attn = jnp.stack(results).reshape(row_count, head_local * DH).astype(jnp.bfloat16)
    width_all = w_out.shape[0]
    attn_wide = attn.astype(jnp.float32)
    first_sum, second_sum = lax.psum(
        (jnp.sum(attn_wide, axis=1), jnp.sum(attn_wide * attn_wide, axis=1)), "head"
    )
    mean = (first_sum / width_all)[:, None]
    square = (second_sum / width_all)[:, None]
    hidden = (
        (attn_wide - mean) * lax.rsqrt(square - mean * mean + 1e-05) * gate_u.astype(jnp.float32)
    )
    hidden = hidden.astype(jnp.bfloat16)
    local_width = head_local * DH
    w_rows = lax.dynamic_slice_in_dim(w_out, lax.axis_index("head") * local_width, local_width, 0)
    summed = lax.psum_scatter(
        jnp.dot(hidden, w_rows, preferred_element_type=jnp.float32),
        "head",
        scatter_dimension=0,
        tiled=True,
    )
    return summed.astype(jnp.bfloat16)


def solution(mesh):
    return jax.shard_map(
        shards,
        mesh=mesh,
        in_specs=(
            P(("req", "head"), None),
            P(None, "head"),
            P(),
            P("req", None, None, None, "head"),
            P("req"),
            P(),
            P("req", None),
        ),
        out_specs=P(("req", "head"), None),
        check_vma=False,
    )
```

profile of v0, /device:TPU:8, one launch (start us, length us, event | category | flops | bytes accessed | tf_op | source)
XLA Modules:
  0.0 321.6 jit_solution(10746997793371658407)
XLA Ops:
  6.5 0.0 copy-start
  6.5 0.0 copy-start.2
  6.5 0.0 copy-start.4
  6.5 0.0 copy-start.5
  6.5 0.0 copy-start.3
  6.5 12.0 %all-to-all-start = ((bf16[1,32,3,128,256]{4,3,2,0,1:T(8,128)(2,1)}), bf16[1,32,3,128,256]{4,3,2,0,1:T(8,128)(2,1)}, u32[]{:S(2)}, u32[]{:S(2)}) async-start(bf16[1,32,3,128,256]{4,3,2,0,1:T(8,128)(2,1)} %bitcast.58), calls=%async_computation | async-start | bytes 12582912 | tf_op jit(solution)/shard_map/all_to_all | solution.py:28
  18.6 0.0 all-gather.2.cloned.1.call-start
  18.6 0.7 all-gather.2.cloned.1.call-update
  19.3 0.0 reduce-scatter.2.cloned.1.call-start
  19.4 0.0 copy-done.2
  19.4 0.1 fusion.26
  19.5 0.1 reduce_window_sum.11
  19.6 0.2 select_reduce_fusion
  19.8 0.0 copy-done.4
  19.8 0.0 copy-done.5
  19.8 0.2 fusion.27
  20.0 0.6 fusion.38
  20.5 0.7 iota_compare_fusion.2
  21.2 0.6 iota_compare_fusion.1
  21.8 28.2 %all-gather.2.cloned.1.call-done = bf16[1024,1024]{1,0:T(8,128)(2,1)} async-done(((bf16[128,1024]{1,0:T(8,128)(2,1)}), bf16[1024,1024]{1,0:T(8,128)(2,1)}) %all-gather.2.cloned.1.call-update) | async-done | bytes 2097168 | tf_op jit(solution)/shard_map/all_gather | solution.py:20
  50.0 2.3 convert_reduce_fusion
  52.2 0.0 copy-done.3
  52.2 2.8 multiply_convert_fusion
  55.1 0.0 copy-start.1
  55.1 0.8 copy-done.1
  55.9 100.5 %all-to-all-done = bf16[1,32,3,128,256]{4,3,2,0,1:T(8,128)(2,1)} async-done(((bf16[1,32,3,128,256]{4,3,2,0,1:T(8,128)(2,1)}), bf16[1,32,3,128,256]{4,3,2,0,1:T(8,128)(2,1)}, u32[]{:S(2)}, u32[]{:S(2)}) %all-to-all-start) | async-done | bytes 6291488 | tf_op jit(solution)/shard_map/all_to_all | solution.py:28
  156.4 5.6 %gather_fusion = bf16[64,128,256]{2,1,0:T(8,128)(2,1)} fusion(bf16[96,128,256]{2,1,0:T(8,128)(2,1)} %bitcast.1, s32[1024]{0:T(1024)S(1)} %pad_clamp_fusion), kind=kCustom, calls=%fused_computation | custom fusion | bytes 8388864 | tf_op jit(solution)/shard_map/gather | solution.py:37
  162.0 15.1 %reshape.81 = bf16[2,4096,2,2,64]{4,3,2,1,0:T(2,128)(2,1)} reshape(bf16[64,128,256]{2,1,0:T(8,128)(2,1)} %gather_fusion) | data formatting | bytes 8388608 | tf_op jit(solution)/shard_map/reshape | solution.py:37
  177.1 19.4 %fusion.37 = (bf16[1,4096,2,1,64]{4,3,2,1,0:T(2,128)(2,1)}, bf16[1,4096,2,1,64]{4,3,2,1,0:T(2,128)(2,1)}, bf16[1,4096,2,1,64]{4,3,2,1,0:T(2,128)(2,1)}, bf16[1,4096,2,1,64]{4,3,2,1,0:T(2,128)(2,1)}) fusion(bf16[2,4096,2,2,64]{4,3,2,1,0:T(2,128)(2,1)} %reshape.81), kind=kLoop, calls=%fused_computation.55 | loop fusion | bytes 8388608 | tf_op jit(solution)/shard_map/slice | solution.py:46
  196.5 9.4 %copy.45 = bf16[1,4096,2,1,64]{1,4,2,3,0:T(8,128)(2,1)} copy(bf16[1,4096,2,1,64]{4,3,2,1,0:T(2,128)(2,1)} %get-tuple-element.11) | data formatting | bytes 2097152
  205.9 9.5 %copy.47 = bf16[1,4096,2,1,64]{1,4,2,3,0:T(8,128)(2,1)} copy(bf16[1,4096,2,1,64]{4,3,2,1,0:T(2,128)(2,1)} %get-tuple-element.13) | data formatting | bytes 2097152
  215.3 8.4 %copy.48 = bf16[1,4096,2,1,64]{1,4,2,3,0:T(8,128)(2,1)S(1)} copy(bf16[1,4096,2,1,64]{4,3,2,1,0:T(2,128)(2,1)} %get-tuple-element.12) | data formatting | bytes 2097152
  223.7 9.4 %copy.50 = bf16[1,4096,2,1,64]{1,4,2,3,0:T(8,128)(2,1)} copy(bf16[1,4096,2,1,64]{4,3,2,1,0:T(2,128)(2,1)} %get-tuple-element.14) | data formatting | bytes 2097152
  233.2 9.0 %fusion.10 = bf16[1,512,2,64]{1,3,2,0:T(8,128)(2,1)S(1)} fusion(pred[4096]{0:T(1024)(128)(4,1)S(1)} %iota_compare_fusion.2, bf16[1,4096,2,1,64]{1,4,2,3,0:T(8,128)(2,1)} %copy.47, bf16[1,4096,2,1,64]{1,4,2,3,0:T(8,128)(2,1)} %copy.45, bf16[1024,2,2,64]{0,3,2,1:T(8,128)(2,1)} %bitcast.63), kind=kOutput, calls=%fused_computation.15 | convolution fusion | flops 1103101952 | bytes 2363392 | tf_op jit(solution)/shard_map/hcp,phd->chd/dot_general | solution.py:54
  242.1 9.3 %fusion.9 = bf16[1,512,2,64]{1,3,2,0:T(8,128)(2,1)} fusion(pred[4096]{0:T(1024)(128)(4,1)S(1)} %iota_compare_fusion.1, bf16[1,4096,2,1,64]{1,4,2,3,0:T(8,128)(2,1)} %copy.50, bf16[1,4096,2,1,64]{1,4,2,3,0:T(8,128)(2,1)S(1)} %copy.48, bf16[1024,2,2,64]{0,3,2,1:T(8,128)(2,1)} %bitcast.64), kind=kOutput, calls=%fused_computation.14 | convolution fusion | flops 1103101952 | bytes 2363392 | tf_op jit(solution)/shard_map/hcp,phd->chd/dot_general | solution.py:54
  251.5 1.0 fusion.36
  252.5 0.9 fusion.22
  253.4 0.4 copy.42
  253.8 0.1 copy.51
  253.9 12.7 %all-reduce = (f32[1024]{0:T(1024)S(1)}, f32[1024]{0:T(1024)S(1)}) all-reduce(f32[1024]{0:T(1024)S(1)} %bitcast.68, f32[1024]{0:T(1024)S(1)} %bitcast.67), channel_id=1, replica_groups=mesh['req'=32,'head'=8] {'head'}, use_global_device_ids=true, to_apply=%region_8.9 | all-reduce | flops 2048 | bytes 16384 | tf_op jit(solution)/shard_map/psum | solution.py:59
  266.6 0.0 copy-done
  266.7 2.7 fusion.20
  269.3 0.0 reduce-scatter.2.cloned.1.call-update
  269.4 43.7 %reduce-scatter.2.cloned.1.call-done = f32[128,1024]{1,0:T(8,128)} async-done(((f32[1024,1024]{1,0:T(8,128)}), f32[128,1024]{1,0:T(8,128)}) %reduce-scatter.2.cloned.1.call-update) | async-done | bytes 524304 | tf_op jit(solution)/shard_map/reduce_scatter | solution.py:70
  313.0 1.8 convert_element_type.60
  (7 shorter events, 0.1 us)
Async XLA Ops:
  6.5 260.1 %copy-start = (bf16[1024,1024]{1,0:T(8,128)(2,1)S(1)}, bf16[1024,1024]{1,0:T(8,128)(2,1)}, u32[]{:S(2)}) copy-start(bf16[1024,1024]{1,0:T(8,128)(2,1)} %param.9) | copy-start | bytes 6291460
  6.5 12.8 %copy-start.2 = (s32[64,1]{0,1:T(1,128)S(1)}, s32[64,1]{0,1:T(1,128)}, u32[]{:S(2)}) copy-start(s32[64,1]{0,1:T(1,128)} %param.13) | copy-start | bytes 772
  6.5 13.2 %copy-start.4 = (s32[64]{0:T(128)S(1)}, s32[64]{0:T(128)}, u32[]{:S(2)}) copy-start(s32[64]{0:T(128)} %param.12) | copy-start | bytes 772
  6.5 13.2 %copy-start.5 = (s32[2]{0:T(128)S(1)}, s32[2]{0:T(128)}, u32[]{:S(2)}) copy-start(s32[2]{0:T(128)} %param.11) | copy-start | bytes 28
  6.5 45.7 %copy-start.3 = (bf16[1024,256]{1,0:T(8,128)(2,1)S(1)}, bf16[1024,256]{1,0:T(8,128)(2,1)}, u32[]{:S(2)}) copy-start(bf16[1024,256]{1,0:T(8,128)(2,1)} %param.8) | copy-start | bytes 1572868
  6.5 149.9 %all-to-all-start = ((bf16[1,32,3,128,256]{4,3,2,0,1:T(8,128)(2,1)}), bf16[1,32,3,128,256]{4,3,2,0,1:T(8,128)(2,1)}, u32[]{:S(2)}, u32[]{:S(2)}) async-start(bf16[1,32,3,128,256]{4,3,2,0,1:T(8,128)(2,1)} %bitcast.58), calls=%async_computation | async-start | bytes 12582912 | tf_op jit(solution)/shard_map/all_to_all | solution.py:28
  18.6 31.4 %all-gather.2.cloned.1.call-start = ((), (), s32[]{:S(2)}) async-start(), calls=%async_computation.2 | async-start | bytes 2359296 | tf_op jit(solution)/shard_map/all_gather | solution.py:20
  19.3 293.7 %reduce-scatter.2.cloned.1.call-start = ((), (), s32[]{:S(2)}) async-start(), calls=%async_computation.3 | async-start | bytes 4718592 | tf_op jit(solution)/shard_map/reduce_scatter | solution.py:70
  55.1 0.8 copy-start.1
Sparse Core Ops, SparseCore 0:
  21.3 28.6 all-gather.1
  269.5 43.5 reduce-scatter.1
where the time goes:
time: 323 us; the launch traced here: 322 us
  waiting for transfers between devices  173 us (54%)
  local copies, waits for them, and re-layouts  78.7 us (24%)
  matrix products  23.8 us (7%)
  between operations  13.6 us (4%)
  blocking collectives  12.7 us (4%)
  starting transfers between devices  12.1 us (4%)
  other arithmetic  7.75 us (2%)
    all_to_all x1, waiting for transfers between devices, shards(): lax.all_to_all(kv_cache, 'req', split_axis=1, concat_axis=0, tiled=True)  101 us
    reduce_scatter x1, waiting for transfers between devices, shards(): lax.psum_scatter(jnp.dot(hidden, w_rows, preferred_element_type=jnp.float...  43.7 us
    unnamed x19, local copies, waits for them, and re-layouts  37.6 us
    all_gather x1, waiting for transfers between devices, shards(): gathered = lax.all_gather(tokens, 'head', axis=0, tiled=True)  28.2 us
    slice x1, local copies, waits for them, and re-layouts, shards(): values = history[slot, :, :, 1]  19.4 us
    dot_general x2, matrix products, shards(): jnp.einsum('hcp,phd->chd', weights, values, preferred_element_type=jnp.fl...  18.3 us
    reshape x1, local copies, waits for them, and re-layouts, shards(): pool[owners * most_slots + rank]  15.1 us
    psum x1, blocking collectives, shards(): lax.psum((jnp.sum(attn_wide, axis=1), jnp.sum(attn_wide * attn_wide, axis...  12.7 us
  transfers between devices with their start and end apart: 3, of which 3 were waited for; matrix products, arithmetic and copies ran while one was open for 2% of the time, Pallas kernels for 0%

commit v1 on v0

--- a/solution.py
+++ b/solution.py
@@ -9,6 +9,11 @@
 MAXB = 32
 
 
+def all_by_exchange(block, name, d):
+    outgoing = jnp.stack([block] * lax.axis_size(name))
+    return jnp.concatenate(lax.all_to_all(outgoing, name, 0, 0), axis=d)
+
+
 def layer_norm(values):
     mean = jnp.mean(values, axis=-1, keepdims=True)
     square = jnp.mean(values * values, axis=-1, keepdims=True)
@@ -17,7 +22,7 @@
 
 def shards(tokens, w_proj, w_out, kv_cache, slot_request, lengths, block_owner):
     head_local = w_proj.shape[1] // (2 * DH)
-    gathered = lax.all_gather(tokens, "head", axis=0, tiled=True)
+    gathered = all_by_exchange(tokens, "head", 0)
     normed = layer_norm(gathered.astype(jnp.float32)).astype(jnp.bfloat16)
     row_count = normed.shape[0]
     slots = row_count // CAND

time: 323 us -> 353 us (1.093)
  blocking collectives: 12.7 us -> 44.4 us
    all_to_all x0 -> x1, blocking collectives: none -> 31.7 us  [all_by_exchange(): return jnp.concatenate(lax.all_to_all(outgoing, name, 0, 0), axis=d)]
    all_gather x1 -> x0, waiting for transfers between devices: 28.2 us -> none  [shards(): gathered = lax.all_gather(tokens, 'head', axis=0, tiled=True)]
    all_to_all x1, waiting for transfers between devices: 101 us -> 127 us  [shards(): lax.all_to_all(kv_cache, 'req', split_axis=1, concat_axis=0, tiled=True)]
  transfers between devices with their start and end apart: 3 -> 2, of which waited for: 3 -> 2; matrix products, arithmetic and copies ran while one was open for 2% -> 2% of each run, Pallas kernels for 0% -> 0%
where the time goes in v1:
time: 353 us; the launch traced here: 351 us
  waiting for transfers between devices  170 us (48%)
  local copies, waits for them, and re-layouts  80 us (23%)
  blocking collectives  44.4 us (13%)
  matrix products  21.9 us (6%)
  between operations  13.6 us (4%)
  starting transfers between devices  11.9 us (3%)
  other arithmetic  9.89 us (3%)
    all_to_all x1, waiting for transfers between devices, shards(): lax.all_to_all(kv_cache, 'req', split_axis=1, concat_axis=0, tiled=True)  127 us
    reduce_scatter x1, waiting for transfers between devices, shards(): lax.psum_scatter(jnp.dot(hidden, w_rows, preferred_element_type=jnp.float...  42.4 us
    unnamed x19, local copies, waits for them, and re-layouts  37.6 us
    all_to_all x1, blocking collectives, all_by_exchange(): return jnp.concatenate(lax.all_to_all(outgoing, name, 0, 0), axis=d)  31.7 us
    slice x1, local copies, waits for them, and re-layouts, shards(): values = history[slot, :, :, 1]  19.4 us
    dot_general x2, matrix products, shards(): jnp.einsum('hcp,phd->chd', weights, values, preferred_element_type=jnp.fl...  18.3 us
    reshape x1, local copies, waits for them, and re-layouts, shards(): pool[owners * most_slots + rank]  15.1 us
    psum x1, blocking collectives, shards(): lax.psum((jnp.sum(attn_wide, axis=1), jnp.sum(attn_wide * attn_wide, axis...  12.7 us
  transfers between devices with their start and end apart: 2, of which 2 were waited for; matrix products, arithmetic and copies ran while one was open for 2% of the time, Pallas kernels for 0%

profile of v1, /device:TPU:8, one launch (start us, length us, event | category | flops | bytes accessed | tf_op | source)
XLA Modules:
  0.0 351.4 jit_solution(5504634274482203315)
XLA Ops:
  6.5 0.0 copy-start
  6.5 1.4 stack.8
  7.9 31.7 %all_to_all.14 = bf16[8,128,1024]{2,1,0:T(8,128)(2,1)} all-to-all(bf16[8,128,1024]{2,1,0:T(8,128)(2,1)S(1)} %stack.8), channel_id=1, replica_groups=mesh['req'=32,'head'=8] {'head'}, dimensions={0} | all-to-all | bytes 4194304 | tf_op jit(solution)/shard_map/all_to_all | solution.py:14
  39.6 0.0 copy-start.2
  39.6 0.0 copy-start.4
  39.6 0.0 copy-start.5
  39.6 11.9 %all-to-all-start = ((bf16[1,32,3,128,256]{4,3,2,0,1:T(8,128)(2,1)}), bf16[1,32,3,128,256]{4,3,2,0,1:T(8,128)(2,1)}, u32[]{:S(2)}, u32[]{:S(2)}) async-start(bf16[1,32,3,128,256]{4,3,2,0,1:T(8,128)(2,1)} %bitcast.75), calls=%async_computation | async-start | bytes 12582912 | tf_op jit(solution)/shard_map/all_to_all | solution.py:33
  51.5 0.0 copy-start.3
  51.5 0.0 reduce-scatter.2.cloned.1.call-start
  51.6 0.0 copy-done.2
  51.6 0.1 fusion.19
  51.7 0.1 reduce_window_sum.11
  51.8 0.2 select_reduce_fusion
  52.0 0.0 copy-done.4
  52.0 0.0 copy-done.5
  52.0 0.2 fusion.22
  52.2 0.6 fusion.33
  52.7 0.7 iota_compare_fusion.2
  53.4 0.6 iota_compare_fusion.1
  54.0 2.3 convert_reduce_fusion
  56.3 2.1 fusion.1
  58.4 0.0 copy-done.3
  58.4 0.9 multiply_convert_fusion
  59.3 0.0 copy-start.1
  59.3 0.8 copy-done.1
  60.2 127.3 %all-to-all-done = bf16[1,32,3,128,256]{4,3,2,0,1:T(8,128)(2,1)} async-done(((bf16[1,32,3,128,256]{4,3,2,0,1:T(8,128)(2,1)}), bf16[1,32,3,128,256]{4,3,2,0,1:T(8,128)(2,1)}, u32[]{:S(2)}, u32[]{:S(2)}) %all-to-all-start) | async-done | bytes 6291488 | tf_op jit(solution)/shard_map/all_to_all | solution.py:33
  187.5 5.6 %gather_fusion = bf16[64,128,256]{2,1,0:T(8,128)(2,1)} fusion(bf16[96,128,256]{2,1,0:T(8,128)(2,1)} %bitcast.1, s32[1024]{0:T(1024)S(1)} %pad_clamp_fusion), kind=kCustom, calls=%fused_computation | custom fusion | bytes 8388864 | tf_op jit(solution)/shard_map/gather | solution.py:42
  193.1 15.1 %reshape.101 = bf16[2,4096,2,2,64]{4,3,2,1,0:T(2,128)(2,1)} reshape(bf16[64,128,256]{2,1,0:T(8,128)(2,1)} %gather_fusion) | data formatting | bytes 8388608 | tf_op jit(solution)/shard_map/reshape | solution.py:42
  208.1 19.4 %fusion.32 = (bf16[1,4096,2,1,64]{4,3,2,1,0:T(2,128)(2,1)}, bf16[1,4096,2,1,64]{4,3,2,1,0:T(2,128)(2,1)}, bf16[1,4096,2,1,64]{4,3,2,1,0:T(2,128)(2,1)}, bf16[1,4096,2,1,64]{4,3,2,1,0:T(2,128)(2,1)}) fusion(bf16[2,4096,2,2,64]{4,3,2,1,0:T(2,128)(2,1)} %reshape.101), kind=kLoop, calls=%fused_computation.53 | loop fusion | bytes 8388608 | tf_op jit(solution)/shard_map/slice | solution.py:51
  227.5 9.4 %copy.45 = bf16[1,4096,2,1,64]{1,4,2,3,0:T(8,128)(2,1)} copy(bf16[1,4096,2,1,64]{4,3,2,1,0:T(2,128)(2,1)} %get-tuple-element.11) | data formatting | bytes 2097152
  237.0 9.5 %copy.47 = bf16[1,4096,2,1,64]{1,4,2,3,0:T(8,128)(2,1)} copy(bf16[1,4096,2,1,64]{4,3,2,1,0:T(2,128)(2,1)} %get-tuple-element.13) | data formatting | bytes 2097152
  246.4 8.4 %copy.48 = bf16[1,4096,2,1,64]{1,4,2,3,0:T(8,128)(2,1)S(1)} copy(bf16[1,4096,2,1,64]{4,3,2,1,0:T(2,128)(2,1)} %get-tuple-element.12) | data formatting | bytes 2097152
  254.8 9.4 %copy.50 = bf16[1,4096,2,1,64]{1,4,2,3,0:T(8,128)(2,1)} copy(bf16[1,4096,2,1,64]{4,3,2,1,0:T(2,128)(2,1)} %get-tuple-element.14) | data formatting | bytes 2097152
  264.2 9.0 %fusion.5 = bf16[1,512,2,64]{1,3,2,0:T(8,128)(2,1)S(1)} fusion(pred[4096]{0:T(1024)(128)(4,1)S(1)} %iota_compare_fusion.2, bf16[1,4096,2,1,64]{1,4,2,3,0:T(8,128)(2,1)} %copy.47, bf16[1,4096,2,1,64]{1,4,2,3,0:T(8,128)(2,1)} %copy.45, bf16[1024,2,2,64]{0,3,2,1:T(8,128)(2,1)} %bitcast.80), kind=kOutput, calls=%fused_computation.11 | convolution fusion | flops 1103101952 | bytes 2363392 | tf_op jit(solution)/shard_map/hcp,phd->chd/dot_general | solution.py:59
  273.2 9.3 %fusion.4 = bf16[1,512,2,64]{1,3,2,0:T(8,128)(2,1)} fusion(pred[4096]{0:T(1024)(128)(4,1)S(1)} %iota_compare_fusion.1, bf16[1,4096,2,1,64]{1,4,2,3,0:T(8,128)(2,1)} %copy.50, bf16[1,4096,2,1,64]{1,4,2,3,0:T(8,128)(2,1)S(1)} %copy.48, bf16[1024,2,2,64]{0,3,2,1:T(8,128)(2,1)} %bitcast.81), kind=kOutput, calls=%fused_computation.10 | convolution fusion | flops 1103101952 | bytes 2363392 | tf_op jit(solution)/shard_map/hcp,phd->chd/dot_general | solution.py:59
  282.5 1.0 fusion.31
  283.5 0.9 fusion.15
  284.5 0.4 copy.42
  284.9 0.1 copy.51
  285.0 12.7 %all-reduce = (f32[1024]{0:T(1024)S(1)}, f32[1024]{0:T(1024)S(1)}) all-reduce(f32[1024]{0:T(1024)S(1)} %bitcast.85, f32[1024]{0:T(1024)S(1)} %bitcast.84), channel_id=1, replica_groups=mesh['req'=32,'head'=8] {'head'}, use_global_device_ids=true, to_apply=%region_8.9 | all-reduce | flops 2048 | bytes 16384 | tf_op jit(solution)/shard_map/psum | solution.py:64
  297.7 0.0 copy-done
  297.7 2.7 fusion.13
  300.4 0.0 reduce-scatter.2.cloned.1.call-update
  300.4 42.4 %reduce-scatter.2.cloned.1.call-done = f32[128,1024]{1,0:T(8,128)} async-done(((f32[1024,1024]{1,0:T(8,128)}), f32[128,1024]{1,0:T(8,128)}) %reduce-scatter.2.cloned.1.call-update) | async-done | bytes 524304 | tf_op jit(solution)/shard_map/reduce_scatter | solution.py:75
  342.8 1.8 convert_element_type.69
  (8 shorter events, 0.1 us)
Async XLA Ops:
  6.5 291.2 %copy-start = (bf16[1024,1024]{1,0:T(8,128)(2,1)S(1)}, bf16[1024,1024]{1,0:T(8,128)(2,1)}, u32[]{:S(2)}) copy-start(bf16[1024,1024]{1,0:T(8,128)(2,1)} %param.9) | copy-start | bytes 6291460
  39.6 12.0 %copy-start.2 = (s32[64,1]{0,1:T(1,128)S(1)}, s32[64,1]{0,1:T(1,128)}, u32[]{:S(2)}) copy-start(s32[64,1]{0,1:T(1,128)} %param.13) | copy-start | bytes 772
  39.6 12.4 %copy-start.4 = (s32[64]{0:T(128)S(1)}, s32[64]{0:T(128)}, u32[]{:S(2)}) copy-start(s32[64]{0:T(128)} %param.12) | copy-start | bytes 772
  39.6 12.4 %copy-start.5 = (s32[2]{0:T(128)S(1)}, s32[2]{0:T(128)}, u32[]{:S(2)}) copy-start(s32[2]{0:T(128)} %param.11) | copy-start | bytes 28
  39.6 147.9 %all-to-all-start = ((bf16[1,32,3,128,256]{4,3,2,0,1:T(8,128)(2,1)}), bf16[1,32,3,128,256]{4,3,2,0,1:T(8,128)(2,1)}, u32[]{:S(2)}, u32[]{:S(2)}) async-start(bf16[1,32,3,128,256]{4,3,2,0,1:T(8,128)(2,1)} %bitcast.75), calls=%async_computation | async-start | bytes 12582912 | tf_op jit(solution)/shard_map/all_to_all | solution.py:33
  51.5 6.9 %copy-start.3 = (bf16[1024,256]{1,0:T(8,128)(2,1)S(1)}, bf16[1024,256]{1,0:T(8,128)(2,1)}, u32[]{:S(2)}) copy-start(bf16[1024,256]{1,0:T(8,128)(2,1)} %param.8) | copy-start | bytes 1572868
  51.5 291.2 %reduce-scatter.2.cloned.1.call-start = ((), (), s32[]{:S(2)}) async-start(), calls=%async_computation.3 | async-start | bytes 4718592 | tf_op jit(solution)/shard_map/reduce_scatter | solution.py:75
  59.3 0.8 copy-start.1
Sparse Core Ops, SparseCore 0:
  300.5 42.1 reduce-scatter.1
